TPU v7x, 32 devices: a whole 2x2x4 slice. The times are simulated.
32 devices in a mesh: groups: 2 (over x), tile: 16 (over z, y, core).
Axes of the slice: x: 2, y: 2, z: 4, core: 2. Of those that a mesh axis runs over, the one named last changes fastest.
Arguments:
- frames: bfloat16 [32, 16, 64, 384], P(('groups', 'tile')), parts along dimension 0, may hold values from -6 to 6
- norm_gain: float32 [384], replicated, may hold values from 0.1 to 1.9
- conv_weight: bfloat16 [3, 3, 3, 384, 384], replicated, may hold values from -0.0625 to 0.0625
- conv_bias: float32 [384], replicated, may hold values from -3 to 3
- up_weight: bfloat16 [384, 4, 4, 192], replicated, may hold values from -0.15625 to 0.15625
- up_bias: float32 [192], replicated, may hold values from -3 to 3
- continues: int32 [8], P('groups'), parts along dimension 0, may hold values from 0 to 1, as said below
- row_extent: int32 [32], P(('groups', 'tile')), parts along dimension 0, may hold values from 1 to 16, as said below
- col_extent: int32 [32], P(('groups', 'tile')), parts along dimension 0, may hold values from 1 to 64, as said below
Outputs:
- upsampled: bfloat16 [32, 32, 128, 192], P(('groups', 'tile')), parts along dimension 0
There are 2 independent parts, one for each index of `groups`. A program takes and returns all parts, laid end to end along the dimension named above; an argument that names none is the same for every part. Nothing has to cross between parts.
Inputs may be any that keep to these rules, and one draw needn't show every extreme that they name: continues[0] and continues[1] are 0; at least one later entry is 1. The valid cells of every latent frame form one rectangle at its first rows and columns, the same for all latent frames; row_extent is 16 except in tile row 1. col_extent is 64 except in tile column 1, in the same rectangle.
All inputs are finite; a program needn't handle non-finite values.
Results may differ from a plain program's by a relative error of at most 0.0048.
Values may be sent and summed in bfloat16 or wider, within the bound.
No kernel may reach another device: no remote copies, remote signals or barrier semaphores. Data moves between devices by JAX's collectives and lax.ppermute only.
A program may use at most 128 MiB of HBM per device.

v0:
```python
import jax
import numpy as np
import jax.numpy as jnp
from jax import lax
from jax.sharding import PartitionSpec as P


TX = 2


EPSILON = 1e-06

DIRECTIONS = ((1, 0), (-1, 0), (0, 1), (0, -1), (1, 1), (-1, -1), (1, -1), (-1, 1))


def activate(values, norm_gain, valid_cells):
    square = jnp.mean(values * values, axis=-1, keepdims=True)
    scaled = values * lax.rsqrt(square + EPSILON) * norm_gain
    return (jax.nn.silu(scaled) * valid_cells[..., None]).astype(jnp.bfloat16)


def latent_step(block, frame_tiles):
    length = lax.axis_size("tile")
    route = [(i, i + frame_tiles) for i in range(length - frame_tiles)]
    return lax.ppermute(block, "tile", route)


def direction_pairs(frame_tiles, step):
    length = lax.axis_size("tile")
    tile_rows = frame_tiles // TX
    step_rows, step_cols = step
    pairs = []
    for i in range(length):
        latent, rest = divmod(i, frame_tiles)
        ty, tx = divmod(rest, TX)
        ty2, tx2 = ty + step_rows, tx + step_cols
        if 0 <= ty2 < tile_rows and 0 <= tx2 < TX:
            pairs.append((i, latent * frame_tiles + ty2 * TX + tx2))
    return pairs


def direction_groups(frame_tiles):
    groups = []
    for step in DIRECTIONS:
        pairs = direction_pairs(frame_tiles, step)
        kind = (abs(step[0]), abs(step[1]))
        for group in groups:
            if group["kind"] != kind:
                continue
            sources = {s for s, _ in group["pairs"]}
            targets = {t for _, t in group["pairs"]}
            if sources.isdisjoint(s for s, _ in pairs) and targets.isdisjoint(t for _, t in pairs):
                group["steps"].append(step)
                group["pairs"] = group["pairs"] + pairs
                break
        else:
            groups.append({"kind": kind, "steps": [step], "pairs": pairs})
    return groups


def in_frame(ty, tx, tile_rows):
    return (ty >= 0) & (ty < tile_rows) & (tx >= 0) & (tx < TX)


def halo_pieces(cells, frame_tiles, latents_ahead):
    length = lax.axis_size("tile")
    tile_rows = frame_tiles // TX
    position = lax.axis_index("tile")
    ty = position % frame_tiles // TX
    tx = position % TX
    height, breadth, channels = cells.shape
    ahead = latents_ahead * frame_tiles
    received = {}
    for group in direction_groups(frame_tiles):
        steps = group["steps"]
        row_at = jnp.int32(0)
        col_at = jnp.int32(0)
        for step in steps:
            sends = in_frame(ty + step[0], tx + step[1], tile_rows)
            row_at = jnp.where(sends, height - 1 if step[0] == 1 else 0, row_at)
            col_at = jnp.where(sends, breadth - 1 if step[1] == 1 else 0, col_at)
        sizes = (1 if steps[0][0] else height, 1 if steps[0][1] else breadth, channels)
        piece = lax.dynamic_slice(cells, (row_at, col_at, jnp.int32(0)), sizes)
        pairs = [(s, t + ahead) for s, t in group["pairs"] if t + ahead < length]
        got = lax.ppermute(piece, "tile", pairs)
        for step in steps:
            if len(steps) == 1:
                received[step] = got
            else:
                gets = in_frame(ty - step[0], tx - step[1], tile_rows)
                received[step] = jnp.where(gets, got, jnp.zeros_like(got))
    return received


def with_halo(cells, received):
    upper = jnp.concatenate([received[(1, 1)], received[(1, 0)], received[(1, -1)]], axis=1)
    middle = jnp.concatenate([received[(0, 1)], cells, received[(0, -1)]], axis=1)
    lower = jnp.concatenate([received[(-1, 1)], received[(-1, 0)], received[(-1, -1)]], axis=1)
    return jnp.concatenate([upper, middle, lower], axis=0)


def halo_exchange(cells, frame_tiles):
    return with_halo(cells, halo_pieces(cells, frame_tiles, 0))


def conv2d(widened, kernel):
    return lax.conv_general_dilated(
        widened[None],
        kernel,
        (1, 1),
        "VALID",
        dimension_numbers=("NHWC", "HWIO", "NHWC"),
        preferred_element_type=jnp.float32,
    )[0]


def up_kernels(up_weight):
    channels, taps_y, taps_x, out_channels = up_weight.shape
    row_taps = ((3, 1), (2, 0))
    col_taps = ((3, None), (1, 2), (None, 0))
    select = np.zeros((2, 2, 3, taps_y * taps_x, 2), np.float32)
    for row_par in range(2):
        for a, ky in enumerate(row_taps[row_par]):
            for b, kx_pair in enumerate(col_taps):
                for col_par, kx in enumerate(kx_pair):
                    if kx is not None:
                        select[row_par, a, b, ky * taps_x + kx, col_par] = 1.0
    select = jnp.asarray(select.reshape(12, taps_y * taps_x, 2), up_weight.dtype)
    flat = up_weight.reshape(channels, taps_y * taps_x, out_channels)
    picked = jnp.einsum("qkr,ckd->qcrd", select, flat, preferred_element_type=jnp.float32)
    picked = picked.astype(up_weight.dtype).reshape(2, 2, 3, channels, 2 * out_channels)
    return [picked[0], picked[1]]


def body(
    frames, norm_gain, conv_weight, conv_bias, up_weight, up_bias, continues, row_extent, col_extent
):
    latents = continues.shape[0]
    frame_tiles = lax.axis_size("tile") // latents
    position = lax.axis_index("tile")
    latent_id = position // frame_tiles
    height = frames.shape[1]
    breadth = frames.shape[2]
    out_channels = up_weight.shape[3]
    rows_in = row_extent[0]
    cols_in = col_extent[0]
    row_ids = jnp.arange(height, dtype=jnp.int32)
    col_ids = jnp.arange(breadth, dtype=jnp.int32)
    valid_cells = ((row_ids[:, None] < rows_in) & (col_ids[None, :] < cols_in)).astype(jnp.float32)
    wide_rows = jnp.arange(-1, height + 1, dtype=jnp.int32)
    wide_cols = jnp.arange(-1, breadth + 1, dtype=jnp.int32)
    row_ok = (wide_rows < rows_in) | ((wide_rows == height) & (rows_in == height))
    col_ok = (wide_cols < cols_in) | ((wide_cols == breadth) & (cols_in == breadth))
    wide_valid = (row_ok[:, None] & col_ok[None, :]).astype(jnp.float32)

    raw = frames[0]
    raw_last = latent_step(raw, frame_tiles)
    halo_own = halo_pieces(raw, frame_tiles, 0)
    kernels = up_kernels(up_weight)
    raw_wide = with_halo(raw, halo_own)
    raw_wide, own_gain, own_valid = lax.optimization_barrier((raw_wide, norm_gain, wide_valid))
    active = activate(raw_wide.astype(jnp.float32), own_gain, own_valid)
    pair_kernel = jnp.concatenate([conv_weight[2], conv_weight[1]], axis=2)
    active, pair_kernel = lax.optimization_barrier((active, pair_kernel))
    raw_before = latent_step(raw_last, frame_tiles)
    halo_last = halo_pieces(raw_last, frame_tiles, 0)
    last_wide = with_halo(raw_last, halo_last)
    last_frame = activate(last_wide.astype(jnp.float32), norm_gain, wide_valid)
    conv_last = conv2d(jnp.concatenate([active, last_frame], axis=-1), pair_kernel)

    slots = jnp.arange(latents, dtype=jnp.int32)
    flag_second = jnp.sum(jnp.where(slots == latent_id, continues, 0)).astype(jnp.bfloat16)
    before_wide = with_halo(raw_before, halo_pieces(raw_before, frame_tiles, 0))
    before = activate(before_wide.astype(jnp.float32), norm_gain, wide_valid) * flag_second
    conv_out = conv2d(before, conv_weight[0]) + conv_last

    values = raw.astype(jnp.float32)
    hidden = ((values + conv_out + conv_bias) * valid_cells[..., None]).astype(jnp.bfloat16)
    hidden_wide = halo_exchange(hidden, frame_tiles)
    bias_pair = jnp.concatenate([up_bias, up_bias])
    planes = []
    for row_par in range(2):
        summed = conv2d(hidden_wide[row_par : row_par + height + 1], kernels[row_par])
        planes.append(((summed + bias_pair) * valid_cells[..., None]).astype(jnp.bfloat16))
    woven = jnp.stack(planes, axis=1)
    upsampled = woven.reshape(2 * height, 2 * breadth, out_channels)
    return upsampled[None]


def solution(mesh):
    return jax.shard_map(
        body,
        mesh=mesh,
        in_specs=(
            P(("groups", "tile"), None, None, None),
            P(),
            P(),
            P(),
            P(),
            P(),
            P("groups"),
            P(("groups", "tile")),
            P(("groups", "tile")),
        ),
        out_specs=P(("groups", "tile"), None, None, None),
        check_vma=False,
    )
```

profile of v0, /device:TPU:11, one launch (start us, length us, event | category | flops | bytes accessed | tf_op | source)
XLA Modules:
  0.0 95.5 jit_solution(14766794437691433107)
XLA Ops:
  0.0 3.2 %collective-permute-start = (bf16[16,64,384]{2,1,0:T(8,128)(2,1)}, bf16[16,64,384]{2,1,0:T(8,128)(2,1)S(1)}, u32[]{:S(2)}, u32[]{:S(2)}) collective-permute-start(bf16[16,64,384]{2,1,0:T(8,128)(2,1)} %bitcast.95), channel_id=1, source_target_pairs={{0,4},{1,5},{2,6},{3,7},{4,8},{5,9},{6,10},{7,11},{8,12},{9,13},{1... | collective-permute-start | bytes 2359304 | tf_op jit(solution)/shard_map/ppermute | solution.py:25
  6.6 1.2 %collective-permute-start.6 = (bf16[1,64,384]{2,1,0:T(8,128)(2,1)S(1)}, bf16[1,64,384]{2,1,0:T(8,128)(2,1)}, u32[]{:S(2)}, u32[]{:S(2)}) collective-permute-start(bf16[1,64,384]{2,1,0:T(8,128)(2,1)S(1)} %dynamic-slice_bitcast_fusion), channel_id=1, source_target_pairs={{0,2},{1,3},{4,6},{5,7},{8,10},{9,11},{12,14},{13,15},{2,0},{3,1},... | collective-permute-start | bytes 147464 | tf_op jit(solution)/shard_map/ppermute | solution.py:85
  7.8 1.3 %fusion.68 = bf16[1,1,384]{2,1,0:T(2,128)(2,1)} fusion(bf16[1,16,64,384]{3,2,1,0:T(8,128)(2,1)} %param.10, s32[]{:T(128)S(6)} %select_n.307, s32[]{:T(128)S(6)} %select_n.311), kind=kLoop, calls=%fused_computation.144 | loop fusion | bytes 1544 | tf_op jit(solution)/shard_map/dynamic_slice | solution.py:83
  10.9 4.9 %slice_bitcast_fusion.1 = (bf16[3,3,384,384]{3,2,1,0:T(8,128)(2,1)S(1)}, bf16[3,3,384,384]{3,2,1,0:T(8,128)(2,1)}) fusion(bf16[3,3,3,384,384]{4,3,2,1,0:T(8,128)(2,1)} %param.12), kind=kLoop, calls=%fused_computation.7 | loop fusion | bytes 10616832 | tf_op jit(solution)/shard_map/squeeze | solution.py:163
  15.8 1.7 %convert_bitcast_fusion = bf16[12,384,2,192]{1,0,3,2:T(8,128)(2,1)S(1)} fusion(bf16[12,16,2,1]{1,0,3,2:T(8,128)(2,1)S(1)} %copy-done.5, bf16[384,16,192]{0,2,1:T(8,128)(2,1)S(1)} %bitcast.97), kind=kOutput, calls=%fused_computation.3 | convolution fusion | flops 58392576 | bytes 5899008 | tf_op jit(solution)/shard_map/qkr,ckd->qcrd/dot_general | solution.py:130
  17.6 3.1 %fusion.82 = (bf16[6,384,2,192]{1,0,3,2:T(8,128)(2,1)}, bf16[6,384,2,192]{1,0,3,2:T(8,128)(2,1)}) fusion(bf16[12,384,2,192]{1,0,3,2:T(8,128)(2,1)S(1)} %convert_bitcast_fusion), kind=kLoop, calls=%fused_computation.160 | loop fusion | bytes 7077888 | tf_op jit(solution)/shard_map/slice | solution.py:132
  21.5 4.7 %pad_maximum_fusion = bf16[3,3,768,384]{3,2,1,0:T(8,128)(2,1)} fusion(bf16[3,3,384,384]{3,2,1,0:T(8,128)(2,1)} %get-tuple-element.18, bf16[3,3,384,384]{3,2,1,0:T(8,128)(2,1)S(1)} %get-tuple-element.17), kind=kLoop, calls=%fused_computation | loop fusion | flops 10616832 | bytes 10616832 | tf_op jit(solution)/shard_map/concatenate | solution.py:163
  27.0 3.3 %copy.53 = bf16[6,384,2,192]{1,3,2,0:T(8,128)(2,1)} copy(bf16[6,384,2,192]{1,0,3,2:T(8,128)(2,1)} %get-tuple-element.20) | data formatting | bytes 3538944 | tf_op jit(solution)/shard_map/slice | solution.py:132
  34.1 1.4 %collective-permute-start.8 = (bf16[1,1,384]{2,1,0:T(2,128)(2,1)S(1)}, bf16[1,1,384]{2,1,0:T(2,128)(2,1)S(1)}, u32[]{:S(2)}, u32[]{:S(2)}) collective-permute-start(bf16[1,1,384]{2,1,0:T(2,128)(2,1)S(1)} %constant_dynamic-slice_fusion.5), channel_id=1, source_target_pairs={{0,3},{4,7},{8,11},{12,15},{3,0},{7,4},{11,8},{15,12},{1,2},{5,6},... | collective-permute-start | bytes 2312 | tf_op jit(solution)/shard_map/ppermute | solution.py:85
  36.4 3.4 %collective-permute-start.1 = (bf16[16,64,384]{2,1,0:T(8,128)(2,1)S(1)}, bf16[16,64,384]{2,1,0:T(8,128)(2,1)S(1)}, u32[]{:S(2)}, u32[]{:S(2)}) collective-permute-start(bf16[16,64,384]{2,1,0:T(8,128)(2,1)S(1)} %collective-permute-done), channel_id=1, source_target_pairs={{0,4},{1,5},{2,6},{3,7},{4,8},{5,9},{6,10},{7,11},{8,12},{9,13},{1... | collective-permute-start | bytes 2359304 | tf_op jit(solution)/shard_map/ppermute | solution.py:25
  42.5 1.0 %slice-done = s8[4194304]{0:T(1024)(128)(4,1)S(1)} async-done(((s8[5308416]{0:T(1024)(128)(4,1)}), s8[4194304]{0:T(1024)(128)(4,1)S(1)}, s32[]{:S(2)}) %slice-start) | async-done | bytes 4194328
  44.0 8.5 %fusion.6 = f32[16,8,9,384]{3,1,2,0:T(8,128)S(1)} fusion(bf16[3,3,768,384]{3,2,1,0:T(8,128)(2,1)S(1)} %bitcast.94, bf16[18,1,7,2,768]{4,2,3,0,1:T(8,128)(2,1)S(1)} %slice.34, bf16[18,1,8,9,768]{4,2,3,0,1:T(8,128)(2,1)S(1)} %copy.40), kind=kOutput, calls=%fused_computation.15 | convolution fusion | flops 6122594304 | bytes 9455616 | tf_op jit(solution)/shard_map/conv_general_dilated | solution.py:107
  52.5 4.8 %collective-permute-done.1 = bf16[16,64,384]{2,1,0:T(8,128)(2,1)S(1)} collective-permute-done((bf16[16,64,384]{2,1,0:T(8,128)(2,1)S(1)}, bf16[16,64,384]{2,1,0:T(8,128)(2,1)S(1)}, u32[]{:S(2)}, u32[]{:S(2)}) %collective-permute-start.1) | collective-permute-done | bytes 786464 | tf_op jit(solution)/shard_map/ppermute | solution.py:25
  57.3 2.0 %collective-permute-start.2 = (bf16[1,1,384]{2,1,0:T(2,128)(2,1)S(1)}, bf16[1,1,384]{2,1,0:T(2,128)(2,1)S(1)}, u32[]{:S(2)}, u32[]{:S(2)}) collective-permute-start(bf16[1,1,384]{2,1,0:T(2,128)(2,1)S(1)} %constant_dynamic-slice_fusion.10), channel_id=1, source_target_pairs={{0,3},{4,7},{8,11},{12,15},{3,0},{7,4},{11,8},{15,12},{1,2},{5,6},... | collective-permute-start | bytes 2312 | tf_op jit(solution)/shard_map/ppermute | solution.py:85
  61.3 1.7 %collective-permute-done.3 = bf16[1,64,384]{2,1,0:T(8,128)(2,1)S(1)} collective-permute-done((bf16[1,64,384]{2,1,0:T(8,128)(2,1)S(1)}, bf16[1,64,384]{2,1,0:T(8,128)(2,1)S(1)}, u32[]{:S(2)}, u32[]{:S(2)}) %collective-permute-start.3) | collective-permute-done | bytes 49184 | tf_op jit(solution)/shard_map/ppermute | solution.py:85
  63.6 1.3 %fusion.64 = bf16[18,1,66,384]{3,2,0,1:T(8,128)(2,1)S(1)} fusion(bf16[1,1,66,384]{3,2,1,0:T(8,128)(2,1)S(1)} %get-tuple-element.58, bf16[1,16,66,384]{3,2,1,0:T(8,128)(2,1)S(1)} %maximum_bitcast_fusion.3, bf16[1,1,66,384]{3,2,1,0:T(8,128)(2,1)S(1)} %get-tuple-element.57, f32[18,66]{1,0:T(8,128)S(1)} %and_convert_fusion, f32[384]{0:T(512)S(1)} %copy-done.4, ...), kind=kLoop, calls=%fused_computation.79 | loop fusion | flops 5474304 | bytes 1835810 | tf_op jit(solution)/shard_map/mul | solution.py:174
  65.9 6.2 %select_add_fusion = f32[16,8,9,384]{3,1,2,0:T(8,128)S(1)} fusion(f32[16,8,9,384]{3,1,2,0:T(8,128)S(1)} %fusion.6, bf16[3,3,3,384,384]{4,3,2,1,0:T(8,128)(2,1)} %param.12, bf16[18,1,7,2,384]{4,2,3,0,1:T(8,128)(2,1)S(1)} %slice.33, bf16[18,1,8,9,384]{4,2,3,0,1:T(8,128)(2,1)S(1)} %copy.35, pred[8,9]{0,1:T(8,128)(4,1)S(1)} %copy-done.9), kind=kOutput, calls=%fused_computation.47 | convolution fusion | flops 3062624256 | bytes 7382088 | tf_op jit(solution)/shard_map/conv_general_dilated | solution.py:107
  74.5 1.3 %collective-permute-start.12 = (bf16[1,64,384]{2,1,0:T(8,128)(2,1)S(1)}, bf16[1,64,384]{2,1,0:T(8,128)(2,1)S(1)}, u32[]{:S(2)}, u32[]{:S(2)}) collective-permute-start(bf16[1,64,384]{2,1,0:T(8,128)(2,1)S(1)} %constant_dynamic-slice_fusion.1), channel_id=1, source_target_pairs={{0,2},{1,3},{4,6},{5,7},{8,10},{9,11},{12,14},{13,15},{2,0},{3,1},... | collective-permute-start | bytes 147464 | tf_op jit(solution)/shard_map/ppermute | solution.py:85
  79.1 1.1 %copy-done.3 = bf16[6,384,2,192]{1,3,2,0:T(8,128)(2,1)S(1)} copy-done((bf16[6,384,2,192]{1,3,2,0:T(8,128)(2,1)S(1)}, bf16[6,384,2,192]{1,3,2,0:T(8,128)(2,1)}, u32[]{:S(2)}) %copy-start.3) | copy-done | bytes 1769496
  80.3 2.9 %convolution_select_fusion = f32[16,8,9,384]{3,1,2,0:T(8,128)S(1)} fusion(bf16[2,3,384,384]{2,3,1,0:T(8,128)(2,1)S(1)} %bitcast.99, bf16[17,1,7,2,384]{4,2,3,0,1:T(8,128)(2,1)S(1)} %slice.39, bf16[17,1,8,9,384]{4,2,3,0,1:T(8,128)(2,1)S(1)} %copy.52, pred[8,9]{0,1:T(8,128)(4,1)S(1)} %copy-done.9), kind=kOutput, calls=%fused_computation.60 | convolution fusion | flops 2042320896 | bytes 4661832 | tf_op jit(solution)/shard_map/conv_general_dilated | solution.py:107
  84.1 3.2 %convolution_select_fusion.1 = f32[16,8,9,384]{3,1,2,0:T(8,128)S(1)} fusion(bf16[2,3,384,384]{2,3,1,0:T(8,128)(2,1)S(1)} %bitcast.98, bf16[17,1,7,2,384]{4,2,3,0,1:T(8,128)(2,1)S(1)} %slice.36, bf16[17,1,8,9,384]{4,2,3,0,1:T(8,128)(2,1)S(1)} %copy.45, pred[8,9]{0,1:T(8,128)(4,1)S(1)} %copy-done.9), kind=kOutput, calls=%fused_computation.61 | convolution fusion | flops 2042320896 | bytes 4661832 | tf_op jit(solution)/shard_map/conv_general_dilated | solution.py:107
  88.2 1.5 %copy.55 = bf16[16,2,64,384]{3,2,1,0:T(8,128)(2,1)} copy(bf16[16,2,64,384]{3,0,2,1:T(8,128)(2,1)S(1)} %pad_maximum_fusion.1) | data formatting | bytes 3145728 | tf_op jit(solution)/shard_map/stack | solution.py:185
  89.7 3.1 %broadcast_in_dim_reshape.3 = bf16[1,32,128,192]{3,2,1,0:T(8,128)(2,1)S(1)} reshape(bf16[16,2,64,384]{3,2,1,0:T(8,128)(2,1)} %copy.55) | data formatting | bytes 3145728 | tf_op jit(solution)/shard_map/broadcast_in_dim;reshape | solution.py:187
  92.8 2.7 %copy.56 = bf16[1,32,128,192]{2,3,1,0:T(8,128)(2,1)} copy(bf16[1,32,128,192]{3,2,1,0:T(8,128)(2,1)S(1)} %broadcast_in_dim_reshape.3) | data formatting | bytes 3145728 | tf_op jit(solution)/shard_map/broadcast_in_dim;reshape | solution.py:187
  (114 shorter events, 23.1 us)
Async XLA Ops:
  0.0 34.0 %collective-permute-start = (bf16[16,64,384]{2,1,0:T(8,128)(2,1)}, bf16[16,64,384]{2,1,0:T(8,128)(2,1)S(1)}, u32[]{:S(2)}, u32[]{:S(2)}) collective-permute-start(bf16[16,64,384]{2,1,0:T(8,128)(2,1)} %bitcast.95), channel_id=1, source_target_pairs={{0,4},{1,5},{2,6},{3,7},{4,8},{5,9},{6,10},{7,11},{8,12},{9,13},{1... | collective-permute-start | bytes 2359304 | tf_op jit(solution)/shard_map/ppermute | solution.py:25
  4.8 25.9 %collective-permute-start.7 = (bf16[16,1,384]{2,1,0:T(2,128)(2,1)}, bf16[16,1,384]{2,1,0:T(2,128)(2,1)}, u32[]{:S(2)}, u32[]{:S(2)}) collective-permute-start(bf16[16,1,384]{2,1,0:T(2,128)(2,1)} %copy.37), channel_id=1, source_target_pairs={{0,1},{2,3},{4,5},{6,7},{8,9},{10,11},{12,13},{14,15},{1,0},{3,2},... | collective-permute-start | bytes 36872 | tf_op jit(solution)/shard_map/ppermute | solution.py:85
  6.6 24.9 %collective-permute-start.6 = (bf16[1,64,384]{2,1,0:T(8,128)(2,1)S(1)}, bf16[1,64,384]{2,1,0:T(8,128)(2,1)}, u32[]{:S(2)}, u32[]{:S(2)}) collective-permute-start(bf16[1,64,384]{2,1,0:T(8,128)(2,1)S(1)} %dynamic-slice_bitcast_fusion), channel_id=1, source_target_pairs={{0,2},{1,3},{4,6},{5,7},{8,10},{9,11},{12,14},{13,15},{2,0},{3,1},... | collective-permute-start | bytes 147464 | tf_op jit(solution)/shard_map/ppermute | solution.py:85
  9.1 21.6 %collective-permute-start.5 = (bf16[1,1,384]{2,1,0:T(2,128)(2,1)}, bf16[1,1,384]{2,1,0:T(2,128)(2,1)S(1)}, u32[]{:S(2)}, u32[]{:S(2)}) collective-permute-start(bf16[1,1,384]{2,1,0:T(2,128)(2,1)} %fusion.68), channel_id=1, source_target_pairs={{0,3},{4,7},{8,11},{12,15},{3,0},{7,4},{11,8},{15,12},{1,2},{5,6},... | collective-permute-start | bytes 2312 | tf_op jit(solution)/shard_map/ppermute | solution.py:85
  10.8 5.0 %copy-start.2 = (bf16[384,4,4,192]{0,3,2,1:T(8,128)(2,1)S(1)}, bf16[384,4,4,192]{0,3,2,1:T(8,128)(2,1)}, u32[]{:S(2)}) copy-start(bf16[384,4,4,192]{0,3,2,1:T(8,128)(2,1)} %param.14) | copy-start | bytes 7077892
  10.8 5.0 %copy-start.5 = (bf16[12,16,2,1]{1,0,3,2:T(8,128)(2,1)S(1)}, bf16[12,16,2,1]{1,0,3,2:T(8,128)(2,1)}, u32[]{:S(2)}) copy-start(bf16[12,16,2,1]{1,0,3,2:T(8,128)(2,1)} %constant.136) | copy-start | bytes 2308
  17.6 3.1 %copy-start.8 = (s32[4]{0:T(128)S(1)}, s32[4]{0:T(128)}, u32[]{:S(2)}) copy-start(s32[4]{0:T(128)} %param.16) | copy-start | bytes 52
  21.5 4.8 %copy-start.7 = (f32[192]{0:T(256)S(1)}, f32[192]{0:T(256)}, u32[]{:S(2)}) copy-start(f32[192]{0:T(256)} %param.15) | copy-start | bytes 2308
  27.0 3.3 %copy-start = (bf16[6,384,2,192]{1,0,3,2:T(8,128)(2,1)S(1)}, bf16[6,384,2,192]{1,0,3,2:T(8,128)(2,1)}, u32[]{:S(2)}) copy-start(bf16[6,384,2,192]{1,0,3,2:T(8,128)(2,1)} %get-tuple-element.19) | copy-start | bytes 5308420
  30.4 2.0 %copy-start.1 = (bf16[1,16,64,384]{3,2,1,0:T(8,128)(2,1)S(1)}, bf16[1,16,64,384]{3,2,1,0:T(8,128)(2,1)}, u32[]{:S(2)}) copy-start(bf16[1,16,64,384]{3,2,1,0:T(8,128)(2,1)} %param.10) | copy-start | bytes 2359300
  30.6 2.7 %copy-start.4 = (f32[384]{0:T(512)S(1)}, f32[384]{0:T(512)}, u32[]{:S(2)}) copy-start(f32[384]{0:T(512)} %param.11) | copy-start | bytes 4612
  34.1 5.7 %collective-permute-start.8 = (bf16[1,1,384]{2,1,0:T(2,128)(2,1)S(1)}, bf16[1,1,384]{2,1,0:T(2,128)(2,1)S(1)}, u32[]{:S(2)}, u32[]{:S(2)}) collective-permute-start(bf16[1,1,384]{2,1,0:T(2,128)(2,1)S(1)} %constant_dynamic-slice_fusion.5), channel_id=1, source_target_pairs={{0,3},{4,7},{8,11},{12,15},{3,0},{7,4},{11,8},{15,12},{1,2},{5,6},... | collective-permute-start | bytes 2312 | tf_op jit(solution)/shard_map/ppermute | solution.py:85
  35.5 4.4 %collective-permute-start.9 = (bf16[1,64,384]{2,1,0:T(8,128)(2,1)S(1)}, bf16[1,64,384]{2,1,0:T(8,128)(2,1)S(1)}, u32[]{:S(2)}, u32[]{:S(2)}) collective-permute-start(bf16[1,64,384]{2,1,0:T(8,128)(2,1)S(1)} %constant_dynamic-slice_fusion.4), channel_id=1, source_target_pairs={{0,2},{1,3},{4,6},{5,7},{8,10},{9,11},{12,14},{13,15},{2,0},{3,1},... | collective-permute-start | bytes 147464 | tf_op jit(solution)/shard_map/ppermute | solution.py:85
  35.7 4.0 %collective-permute-start.10 = (bf16[16,1,384]{2,1,0:T(2,128)(2,1)S(1)}, bf16[16,1,384]{2,1,0:T(2,128)(2,1)S(1)}, u32[]{:S(2)}, u32[]{:S(2)}) collective-permute-start(bf16[16,1,384]{2,1,0:T(2,128)(2,1)S(1)} %constant_dynamic-slice_fusion.3), channel_id=1, source_target_pairs={{0,1},{2,3},{4,5},{6,7},{8,9},{10,11},{12,13},{14,15},{1,0},{3,2},... | collective-permute-start | bytes 36872 | tf_op jit(solution)/shard_map/ppermute | solution.py:85
  36.4 21.0 %collective-permute-start.1 = (bf16[16,64,384]{2,1,0:T(8,128)(2,1)S(1)}, bf16[16,64,384]{2,1,0:T(8,128)(2,1)S(1)}, u32[]{:S(2)}, u32[]{:S(2)}) collective-permute-start(bf16[16,64,384]{2,1,0:T(8,128)(2,1)S(1)} %collective-permute-done), channel_id=1, source_target_pairs={{0,4},{1,5},{2,6},{3,7},{4,8},{5,9},{6,10},{7,11},{8,12},{9,13},{1... | collective-permute-start | bytes 2359304 | tf_op jit(solution)/shard_map/ppermute | solution.py:25
  41.3 2.2 %slice-start = ((s8[5308416]{0:T(1024)(128)(4,1)}), s8[4194304]{0:T(1024)(128)(4,1)S(1)}, s32[]{:S(2)}) async-start(s8[5308416]{0:T(1024)(128)(4,1)} %bitcast.93), calls=%async_computation | async-start | bytes 8388608
  41.8 2.2 %slice-start.1 = ((s8[5308416]{0:T(1024)(128)(4,1)}), s8[1114112]{0:T(1024)(128)(4,1)S(1)}, s32[]{:S(2)}) async-start(s8[5308416]{0:T(1024)(128)(4,1)} %bitcast.93), calls=%async_computation.1 | async-start | bytes 2228224
  57.3 3.5 %collective-permute-start.2 = (bf16[1,1,384]{2,1,0:T(2,128)(2,1)S(1)}, bf16[1,1,384]{2,1,0:T(2,128)(2,1)S(1)}, u32[]{:S(2)}, u32[]{:S(2)}) collective-permute-start(bf16[1,1,384]{2,1,0:T(2,128)(2,1)S(1)} %constant_dynamic-slice_fusion.10), channel_id=1, source_target_pairs={{0,3},{4,7},{8,11},{12,15},{3,0},{7,4},{11,8},{15,12},{1,2},{5,6},... | collective-permute-start | bytes 2312 | tf_op jit(solution)/shard_map/ppermute | solution.py:85
  59.3 3.7 %collective-permute-start.3 = (bf16[1,64,384]{2,1,0:T(8,128)(2,1)S(1)}, bf16[1,64,384]{2,1,0:T(8,128)(2,1)S(1)}, u32[]{:S(2)}, u32[]{:S(2)}) collective-permute-start(bf16[1,64,384]{2,1,0:T(8,128)(2,1)S(1)} %constant_dynamic-slice_fusion.9), channel_id=1, source_target_pairs={{0,2},{1,3},{4,6},{5,7},{8,10},{9,11},{12,14},{13,15},{2,0},{3,1},... | collective-permute-start | bytes 147464 | tf_op jit(solution)/shard_map/ppermute | solution.py:85
  59.6 1.3 %collective-permute-start.4 = (bf16[16,1,384]{2,1,0:T(2,128)(2,1)S(1)}, bf16[16,1,384]{2,1,0:T(2,128)(2,1)S(1)}, u32[]{:S(2)}, u32[]{:S(2)}) collective-permute-start(bf16[16,1,384]{2,1,0:T(2,128)(2,1)S(1)} %constant_dynamic-slice_fusion.8), channel_id=1, source_target_pairs={{0,1},{2,3},{4,5},{6,7},{8,9},{10,11},{12,13},{14,15},{1,0},{3,2},... | collective-permute-start | bytes 36872 | tf_op jit(solution)/shard_map/ppermute | solution.py:85
  73.8 3.2 %collective-permute-start.11 = (bf16[1,1,384]{2,1,0:T(2,128)(2,1)S(1)}, bf16[1,1,384]{2,1,0:T(2,128)(2,1)S(1)}, u32[]{:S(2)}, u32[]{:S(2)}) collective-permute-start(bf16[1,1,384]{2,1,0:T(2,128)(2,1)S(1)} %constant_dynamic-slice_fusion.2), channel_id=1, source_target_pairs={{0,3},{4,7},{8,11},{12,15},{3,0},{7,4},{11,8},{15,12},{1,2},{5,6},... | collective-permute-start | bytes 2312 | tf_op jit(solution)/shard_map/ppermute | solution.py:85
  74.5 3.5 %collective-permute-start.12 = (bf16[1,64,384]{2,1,0:T(8,128)(2,1)S(1)}, bf16[1,64,384]{2,1,0:T(8,128)(2,1)S(1)}, u32[]{:S(2)}, u32[]{:S(2)}) collective-permute-start(bf16[1,64,384]{2,1,0:T(8,128)(2,1)S(1)} %constant_dynamic-slice_fusion.1), channel_id=1, source_target_pairs={{0,2},{1,3},{4,6},{5,7},{8,10},{9,11},{12,14},{13,15},{2,0},{3,1},... | collective-permute-start | bytes 147464 | tf_op jit(solution)/shard_map/ppermute | solution.py:85
  75.8 1.2 %collective-permute-start.13 = (bf16[16,1,384]{2,1,0:T(2,128)(2,1)S(1)}, bf16[16,1,384]{2,1,0:T(2,128)(2,1)S(1)}, u32[]{:S(2)}, u32[]{:S(2)}) collective-permute-start(bf16[16,1,384]{2,1,0:T(2,128)(2,1)S(1)} %constant_dynamic-slice_fusion), channel_id=1, source_target_pairs={{0,1},{2,3},{4,5},{6,7},{8,9},{10,11},{12,13},{14,15},{1,0},{3,2},... | collective-permute-start | bytes 36872 | tf_op jit(solution)/shard_map/ppermute | solution.py:85
  78.8 1.5 %copy-start.3 = (bf16[6,384,2,192]{1,3,2,0:T(8,128)(2,1)S(1)}, bf16[6,384,2,192]{1,3,2,0:T(8,128)(2,1)}, u32[]{:S(2)}) copy-start(bf16[6,384,2,192]{1,3,2,0:T(8,128)(2,1)} %copy.53) | copy-start | bytes 5308420
  (2 other events, 1.4 us)
where the time goes:
time: 96.8 us; the launch traced here: 95.5 us
  local copies, waits for them, and re-layouts  30.2 us (31%)
  matrix products  22.6 us (23%)
  starting transfers between devices  16.3 us (17%)
  other arithmetic  14.5 us (15%)
  waiting for transfers between devices  9.22 us (10%)
  between operations  2.67 us (3%)
    conv_general_dilated x4, matrix products, conv2d(): lax.conv_general_dilated(widened[None], kernel, (1, 1), 'VALID', dimensio...  20.9 us
    ppermute x12, starting transfers between devices, halo_pieces(): got = lax.ppermute(piece, 'tile', pairs)  9.69 us
    slice x3, local copies, waits for them, and re-layouts, up_kernels(): return [picked[0], picked[1]]  6.67 us
    ppermute x2, starting transfers between devices, latent_step(): return lax.ppermute(block, 'tile', route)  6.57 us
    another operation x2, local copies, waits for them, and re-layouts, body(): return upsampled[None]  5.8 us
    squeeze x1, local copies, waits for them, and re-layouts, body(): pair_kernel = jnp.concatenate([conv_weight[2], conv_weight[1]], axis=2)  4.93 us
    ppermute x2, waiting for transfers between devices, latent_step(): return lax.ppermute(block, 'tile', route)  4.82 us
    concatenate x1, other arithmetic, body(): pair_kernel = jnp.concatenate([conv_weight[2], conv_weight[1]], axis=2)  4.69 us
  transfers between devices with their start and end apart: 14, of which 5 were waited for; matrix products, arithmetic and copies ran while one was open for 40% of the time, Pallas kernels for 0%

commit v1 on v0

--- a/solution.py
+++ b/solution.py
@@ -160,17 +160,19 @@
     raw_wide = with_halo(raw, halo_own)
     raw_wide, own_gain, own_valid = lax.optimization_barrier((raw_wide, norm_gain, wide_valid))
     active = activate(raw_wide.astype(jnp.float32), own_gain, own_valid)
-    pair_kernel = jnp.concatenate([conv_weight[2], conv_weight[1]], axis=2)
+    pair_kernel = jnp.transpose(conv_weight[1:], (1, 2, 0, 3, 4))
+    pair_kernel = pair_kernel.reshape(3, 3, -1, conv_weight.shape[-1])
     active, pair_kernel = lax.optimization_barrier((active, pair_kernel))
     raw_before = latent_step(raw_last, frame_tiles)
     halo_last = halo_pieces(raw_last, frame_tiles, 0)
     last_wide = with_halo(raw_last, halo_last)
     last_frame = activate(last_wide.astype(jnp.float32), norm_gain, wide_valid)
-    conv_last = conv2d(jnp.concatenate([active, last_frame], axis=-1), pair_kernel)
+    conv_last = conv2d(jnp.concatenate([last_frame, active], axis=-1), pair_kernel)
 
     slots = jnp.arange(latents, dtype=jnp.int32)
     flag_second = jnp.sum(jnp.where(slots == latent_id, continues, 0)).astype(jnp.bfloat16)
-    before_wide = with_halo(raw_before, halo_pieces(raw_before, frame_tiles, 0))
+    halo_before = halo_pieces(raw_before, frame_tiles, 0)
+    before_wide = with_halo(raw_before, halo_before)
     before = activate(before_wide.astype(jnp.float32), norm_gain, wide_valid) * flag_second
     conv_out = conv2d(before, conv_weight[0]) + conv_last
 

time: 96.8 us -> 92.4 us (0.955)
  other arithmetic: 14.5 us -> 9.33 us
  local copies, waits for them, and re-layouts: 30.2 us -> 31.8 us
    squeeze x1 -> x0, local copies, waits for them, and re-layouts: 4.93 us -> none  [body(): pair_kernel = jnp.concatenate([conv_weight[2], conv_weight[1]], axis=2)]
    concatenate x1 -> x0, other arithmetic: 4.69 us -> none  [body(): pair_kernel = jnp.concatenate([conv_weight[2], conv_weight[1]], axis=2)]
    unnamed x29 -> x32, local copies, waits for them, and re-layouts: 4.64 us -> 8.69 us
    slice x0 -> x2, local copies, waits for them, and re-layouts: none -> 2.5 us  [body(): pair_kernel = jnp.transpose(conv_weight[1:], (1, 2, 0, 3, 4))]
    conv_general_dilated x4, matrix products: 20.9 us -> 19.1 us  [conv2d(): lax.conv_general_dilated(widened[None], kernel, (1, 1), 'VALID', dimensio...]
    dot_general x1, matrix products: 1.74 us -> 3.42 us  [up_kernels(): jnp.einsum('qkr,ckd->qcrd', select, flat, preferred_element_type=jnp.floa...]
    select_n x12, other arithmetic: 1.84 us -> 0.31 us  [halo_pieces(): received[step] = jnp.where(gets, got, jnp.zeros_like(got))]
    slice x3, local copies, waits for them, and re-layouts: 6.67 us -> 5.47 us  [up_kernels(): return [picked[0], picked[1]]]
  transfers between devices with their start and end apart: 14 -> 14, of which waited for: 5 -> 5; matrix products, arithmetic and copies ran while one was open for 40% -> 35% of each run, Pallas kernels for 0% -> 0%
where the time goes in v1:
time: 92.4 us; the launch traced here: 90.9 us
  local copies, waits for them, and re-layouts  31.8 us (34%)
  matrix products  22.5 us (24%)
  starting transfers between devices  16.3 us (18%)
  other arithmetic  9.33 us (10%)
  waiting for transfers between devices  8.34 us (9%)
  between operations  2.57 us (3%)
    conv_general_dilated x4, matrix products, conv2d(): lax.conv_general_dilated(widened[None], kernel, (1, 1), 'VALID', dimensio...  19.1 us
    ppermute x12, starting transfers between devices, halo_pieces(): got = lax.ppermute(piece, 'tile', pairs)  9.74 us
    unnamed x32, local copies, waits for them, and re-layouts  8.69 us
    ppermute x2, starting transfers between devices, latent_step(): return lax.ppermute(block, 'tile', route)  6.57 us
    another operation x2, local copies, waits for them, and re-layouts, body(): return upsampled[None]  5.8 us
    slice x3, local copies, waits for them, and re-layouts, up_kernels(): return [picked[0], picked[1]]  5.47 us
    dynamic_slice x13, local copies, waits for them, and re-layouts, halo_pieces(): piece = lax.dynamic_slice(cells, (row_at, col_at, jnp.int32(0)), sizes)  4.99 us
    ppermute x12, waiting for transfers between devices, halo_pieces(): got = lax.ppermute(piece, 'tile', pairs)  4.4 us
  transfers between devices with their start and end apart: 14, of which 5 were waited for; matrix products, arithmetic and copies ran while one was open for 35% of the time, Pallas kernels for 0%

profile of v1, /device:TPU:11, one launch (start us, length us, event | category | flops | bytes accessed | tf_op | source)
XLA Modules:
  0.0 90.9 jit_solution(15179406322995551562)
XLA Ops:
  0.0 3.2 %collective-permute-start = (bf16[16,64,384]{2,1,0:T(8,128)(2,1)}, bf16[16,64,384]{2,1,0:T(8,128)(2,1)}, u32[]{:S(2)}, u32[]{:S(2)}) collective-permute-start(bf16[16,64,384]{2,1,0:T(8,128)(2,1)} %bitcast.97), channel_id=1, source_target_pairs={{0,4},{1,5},{2,6},{3,7},{4,8},{5,9},{6,10},{7,11},{8,12},{9,13},{1... | collective-permute-start | bytes 2359304 | tf_op jit(solution)/shard_map/ppermute | solution.py:25
  6.1 1.2 %collective-permute-start.9 = (bf16[1,64,384]{2,1,0:T(8,128)(2,1)S(1)}, bf16[1,64,384]{2,1,0:T(8,128)(2,1)S(1)}, u32[]{:S(2)}, u32[]{:S(2)}) collective-permute-start(bf16[1,64,384]{2,1,0:T(8,128)(2,1)S(1)} %dynamic-slice_bitcast_fusion), channel_id=1, source_target_pairs={{0,2},{1,3},{4,6},{5,7},{8,10},{9,11},{12,14},{13,15},{2,0},{3,1},... | collective-permute-start | bytes 147464 | tf_op jit(solution)/shard_map/ppermute | solution.py:85
  9.8 3.4 %convert_bitcast_fusion = bf16[12,384,2,192]{1,0,3,2:T(8,128)(2,1)S(1)} fusion(bf16[12,16,2,1]{1,0,3,2:T(8,128)(2,1)} %constant.136, bf16[384,16,192]{0,2,1:T(8,128)(2,1)} %bitcast.99), kind=kOutput, calls=%fused_computation.2 | convolution fusion | flops 58392576 | bytes 5899008 | tf_op jit(solution)/shard_map/qkr,ckd->qcrd/dot_general | solution.py:130
  13.2 2.4 %fusion.82 = (bf16[6,384,2,192]{1,0,3,2:T(8,128)(2,1)S(1)}, bf16[6,384,2,192]{1,0,3,2:T(8,128)(2,1)}) fusion(bf16[12,384,2,192]{1,0,3,2:T(8,128)(2,1)S(1)} %convert_bitcast_fusion), kind=kLoop, calls=%fused_computation.157 | loop fusion | bytes 7077888 | tf_op jit(solution)/shard_map/slice | solution.py:132
  17.1 2.5 %slice-done.2 = bf16[2,3,3,384,384]{4,3,2,1,0:T(8,128)(2,1)S(1)} async-done(((bf16[3,3,3,384,384]{4,3,2,1,0:T(8,128)(2,1)}), bf16[2,3,3,384,384]{4,3,2,1,0:T(8,128)(2,1)S(1)}, s32[]{:S(2)}) %slice-start.2) | async-done | bytes 5308440 | tf_op jit(solution)/shard_map/slice | solution.py:163
  19.6 3.0 %copy.61 = bf16[2,3,3,384,384]{4,3,0,2,1:T(8,128)(2,1)} copy(bf16[2,3,3,384,384]{4,3,2,1,0:T(8,128)(2,1)S(1)} %slice-done.2) | data formatting | bytes 10616832
  22.6 1.6 %copy.55 = bf16[6,384,2,192]{1,3,2,0:T(8,128)(2,1)} copy(bf16[6,384,2,192]{1,0,3,2:T(8,128)(2,1)S(1)} %copy-done) | data formatting | bytes 3538944 | tf_op jit(solution)/shard_map/slice | solution.py:132
  24.1 1.5 %copy.49 = bf16[6,384,2,192]{1,3,2,0:T(8,128)(2,1)} copy(bf16[6,384,2,192]{1,0,3,2:T(8,128)(2,1)S(1)} %get-tuple-element.17) | data formatting | bytes 3538944 | tf_op jit(solution)/shard_map/slice | solution.py:132
  28.2 1.3 %collective-permute-start.5 = (bf16[1,1,384]{2,1,0:T(2,128)(2,1)S(1)}, bf16[1,1,384]{2,1,0:T(2,128)(2,1)S(1)}, u32[]{:S(2)}, u32[]{:S(2)}) collective-permute-start(bf16[1,1,384]{2,1,0:T(2,128)(2,1)S(1)} %constant_dynamic-slice_fusion.7), channel_id=1, source_target_pairs={{0,3},{4,7},{8,11},{12,15},{3,0},{7,4},{11,8},{15,12},{1,2},{5,6},... | collective-permute-start | bytes 2312 | tf_op jit(solution)/shard_map/ppermute | solution.py:85
  32.1 3.4 %collective-permute-start.1 = (bf16[16,64,384]{2,1,0:T(8,128)(2,1)}, bf16[16,64,384]{2,1,0:T(8,128)(2,1)S(1)}, u32[]{:S(2)}, u32[]{:S(2)}) collective-permute-start(bf16[16,64,384]{2,1,0:T(8,128)(2,1)} %collective-permute-done), channel_id=1, source_target_pairs={{0,4},{1,5},{2,6},{3,7},{4,8},{5,9},{6,10},{7,11},{8,12},{9,13},{1... | collective-permute-start | bytes 2359304 | tf_op jit(solution)/shard_map/ppermute | solution.py:25
  35.7 1.7 %fusion.16 = (f32[18,66]{1,0:T(8,128)S(1)}, bf16[18,66,384]{2,1,0:T(8,128)(2,1)S(1)}) fusion(bf16[1,1,384]{2,1,0:T(2,128)(2,1)S(1)} %get-tuple-element.48, bf16[1,64,384]{2,1,0:T(8,128)(2,1)S(1)} %get-tuple-element.26, bf16[1,1,384]{2,1,0:T(2,128)(2,1)S(1)} %get-tuple-element.49, bf16[16,1,384]{2,1,0:T(2,128)(2,1)S(1)} %get-tuple-element.36, ...), kind=kLoop, calls=%fused_computation.23 | loop fusion | flops 9578844 | bytes 1829520 | tf_op jit(solution)/shard_map/reduce_sum | solution.py:17
  40.9 8.5 %fusion.6 = f32[16,8,9,384]{3,1,2,0:T(8,128)S(1)} fusion(bf16[3,3,768,384]{3,2,1,0:T(8,128)(2,1)S(1)} %bitcast.96, bf16[18,1,7,2,768]{4,2,3,0,1:T(8,128)(2,1)S(1)} %slice.30, bf16[18,1,8,9,768]{4,2,3,0,1:T(8,128)(2,1)S(1)} %copy.42), kind=kOutput, calls=%fused_computation.12 | convolution fusion | flops 6122594304 | bytes 9455616 | tf_op jit(solution)/shard_map/conv_general_dilated | solution.py:107
  49.4 3.9 %collective-permute-done.1 = bf16[16,64,384]{2,1,0:T(8,128)(2,1)S(1)} collective-permute-done((bf16[16,64,384]{2,1,0:T(8,128)(2,1)}, bf16[16,64,384]{2,1,0:T(8,128)(2,1)S(1)}, u32[]{:S(2)}, u32[]{:S(2)}) %collective-permute-start.1) | collective-permute-done | bytes 786464 | tf_op jit(solution)/shard_map/ppermute | solution.py:25
  53.3 2.0 %collective-permute-start.2 = (bf16[1,1,384]{2,1,0:T(2,128)(2,1)S(1)}, bf16[1,1,384]{2,1,0:T(2,128)(2,1)S(1)}, u32[]{:S(2)}, u32[]{:S(2)}) collective-permute-start(bf16[1,1,384]{2,1,0:T(2,128)(2,1)S(1)} %constant_dynamic-slice_fusion.10), channel_id=1, source_target_pairs={{0,3},{4,7},{8,11},{12,15},{3,0},{7,4},{11,8},{15,12},{1,2},{5,6},... | collective-permute-start | bytes 2312 | tf_op jit(solution)/shard_map/ppermute | solution.py:85
  57.3 1.7 %collective-permute-done.3 = bf16[1,64,384]{2,1,0:T(8,128)(2,1)S(1)} collective-permute-done((bf16[1,64,384]{2,1,0:T(8,128)(2,1)S(1)}, bf16[1,64,384]{2,1,0:T(8,128)(2,1)S(1)}, u32[]{:S(2)}, u32[]{:S(2)}) %collective-permute-start.3) | collective-permute-done | bytes 49184 | tf_op jit(solution)/shard_map/ppermute | solution.py:85
  59.6 1.3 %fusion.64 = bf16[18,1,66,384]{3,2,0,1:T(8,128)(2,1)S(1)} fusion(bf16[1,1,66,384]{3,2,1,0:T(8,128)(2,1)S(1)} %get-tuple-element.56, bf16[1,16,66,384]{3,2,1,0:T(8,128)(2,1)S(1)} %maximum_bitcast_fusion.3, bf16[1,1,66,384]{3,2,1,0:T(8,128)(2,1)S(1)} %get-tuple-element.55, f32[18,66]{1,0:T(8,128)S(1)} %and_convert_fusion, f32[384]{0:T(512)S(1)} %copy-done.4, ...), kind=kLoop, calls=%fused_computation.76 | loop fusion | flops 5474304 | bytes 1835810 | tf_op jit(solution)/shard_map/mul | solution.py:176
  61.9 4.5 %select_add_fusion = f32[16,8,9,384]{3,1,2,0:T(8,128)S(1)} fusion(f32[16,8,9,384]{3,1,2,0:T(8,128)S(1)} %fusion.6, bf16[3,3,3,384,384]{4,3,2,1,0:T(8,128)(2,1)S(1)} %bitcast.86, bf16[18,1,7,2,384]{4,2,3,0,1:T(8,128)(2,1)S(1)} %slice.29, bf16[18,1,8,9,384]{4,2,3,0,1:T(8,128)(2,1)S(1)} %copy.36, pred[8,9]{0,1:T(8,128)(4,1)S(1)} %copy-done.8), kind=kOutput, calls=%fused_computation.44 | convolution fusion | flops 3062624256 | bytes 7411712 | tf_op jit(solution)/shard_map/conv_general_dilated | solution.py:107
  68.8 1.3 %collective-permute-start.12 = (bf16[1,64,384]{2,1,0:T(8,128)(2,1)S(1)}, bf16[1,64,384]{2,1,0:T(8,128)(2,1)S(1)}, u32[]{:S(2)}, u32[]{:S(2)}) collective-permute-start(bf16[1,64,384]{2,1,0:T(8,128)(2,1)S(1)} %constant_dynamic-slice_fusion.1), channel_id=1, source_target_pairs={{0,2},{1,3},{4,6},{5,7},{8,10},{9,11},{12,14},{13,15},{2,0},{3,1},... | collective-permute-start | bytes 147464 | tf_op jit(solution)/shard_map/ppermute | solution.py:85
  73.4 1.1 %copy-done.3 = bf16[6,384,2,192]{1,3,2,0:T(8,128)(2,1)S(1)} copy-done((bf16[6,384,2,192]{1,3,2,0:T(8,128)(2,1)S(1)}, bf16[6,384,2,192]{1,3,2,0:T(8,128)(2,1)}, u32[]{:S(2)}) %copy-start.3) | copy-done | bytes 1769496
  74.5 2.9 %convolution_select_fusion = f32[16,8,9,384]{3,1,2,0:T(8,128)S(1)} fusion(bf16[2,3,384,384]{2,3,1,0:T(8,128)(2,1)S(1)} %bitcast.101, bf16[17,1,7,2,384]{4,2,3,0,1:T(8,128)(2,1)S(1)} %slice.35, bf16[17,1,8,9,384]{4,2,3,0,1:T(8,128)(2,1)S(1)} %copy.54, pred[8,9]{0,1:T(8,128)(4,1)S(1)} %copy-done.8), kind=kOutput, calls=%fused_computation.57 | convolution fusion | flops 2042320896 | bytes 4661832 | tf_op jit(solution)/shard_map/conv_general_dilated | solution.py:107
  79.4 3.2 %convolution_select_fusion.1 = f32[16,8,9,384]{3,1,2,0:T(8,128)S(1)} fusion(bf16[2,3,384,384]{2,3,1,0:T(8,128)(2,1)S(1)} %bitcast.100, bf16[17,1,7,2,384]{4,2,3,0,1:T(8,128)(2,1)S(1)} %slice.32, bf16[17,1,8,9,384]{4,2,3,0,1:T(8,128)(2,1)S(1)} %copy.47, pred[8,9]{0,1:T(8,128)(4,1)S(1)} %copy-done.8), kind=kOutput, calls=%fused_computation.58 | convolution fusion | flops 2042320896 | bytes 4661832 | tf_op jit(solution)/shard_map/conv_general_dilated | solution.py:107
  83.6 1.5 %copy.57 = bf16[16,2,64,384]{3,2,1,0:T(8,128)(2,1)} copy(bf16[16,2,64,384]{3,0,2,1:T(8,128)(2,1)S(1)} %pad_maximum_fusion) | data formatting | bytes 3145728 | tf_op jit(solution)/shard_map/stack | solution.py:187
  85.1 3.1 %broadcast_in_dim_reshape.3 = bf16[1,32,128,192]{3,2,1,0:T(8,128)(2,1)S(1)} reshape(bf16[16,2,64,384]{3,2,1,0:T(8,128)(2,1)} %copy.57) | data formatting | bytes 3145728 | tf_op jit(solution)/shard_map/broadcast_in_dim;reshape | solution.py:189
  88.2 2.7 %copy.58 = bf16[1,32,128,192]{2,3,1,0:T(8,128)(2,1)} copy(bf16[1,32,128,192]{3,2,1,0:T(8,128)(2,1)S(1)} %broadcast_in_dim_reshape.3) | data formatting | bytes 3145728 | tf_op jit(solution)/shard_map/broadcast_in_dim;reshape | solution.py:189
  (118 shorter events, 25.4 us)
Async XLA Ops:
  0.0 27.5 %collective-permute-start = (bf16[16,64,384]{2,1,0:T(8,128)(2,1)}, bf16[16,64,384]{2,1,0:T(8,128)(2,1)}, u32[]{:S(2)}, u32[]{:S(2)}) collective-permute-start(bf16[16,64,384]{2,1,0:T(8,128)(2,1)} %bitcast.97), channel_id=1, source_target_pairs={{0,4},{1,5},{2,6},{3,7},{4,8},{5,9},{6,10},{7,11},{8,12},{9,13},{1... | collective-permute-start | bytes 2359304 | tf_op jit(solution)/shard_map/ppermute | solution.py:25
  4.2 21.5 %collective-permute-start.10 = (bf16[16,1,384]{2,1,0:T(2,128)(2,1)S(1)}, bf16[16,1,384]{2,1,0:T(2,128)(2,1)S(1)}, u32[]{:S(2)}, u32[]{:S(2)}) collective-permute-start(bf16[16,1,384]{2,1,0:T(2,128)(2,1)S(1)} %copy.38), channel_id=1, source_target_pairs={{0,1},{2,3},{4,5},{6,7},{8,9},{10,11},{12,13},{14,15},{1,0},{3,2},... | collective-permute-start | bytes 36872 | tf_op jit(solution)/shard_map/ppermute | solution.py:85
  6.1 19.7 %collective-permute-start.9 = (bf16[1,64,384]{2,1,0:T(8,128)(2,1)S(1)}, bf16[1,64,384]{2,1,0:T(8,128)(2,1)S(1)}, u32[]{:S(2)}, u32[]{:S(2)}) collective-permute-start(bf16[1,64,384]{2,1,0:T(8,128)(2,1)S(1)} %dynamic-slice_bitcast_fusion), channel_id=1, source_target_pairs={{0,2},{1,3},{4,6},{5,7},{8,10},{9,11},{12,14},{13,15},{2,0},{3,1},... | collective-permute-start | bytes 147464 | tf_op jit(solution)/shard_map/ppermute | solution.py:85
  8.0 17.7 %collective-permute-start.8 = (bf16[1,1,384]{2,1,0:T(2,128)(2,1)S(1)}, bf16[1,1,384]{2,1,0:T(2,128)(2,1)S(1)}, u32[]{:S(2)}, u32[]{:S(2)}) collective-permute-start(bf16[1,1,384]{2,1,0:T(2,128)(2,1)S(1)} %fusion.68), channel_id=1, source_target_pairs={{0,3},{4,7},{8,11},{12,15},{3,0},{7,4},{11,8},{15,12},{1,2},{5,6},... | collective-permute-start | bytes 2312 | tf_op jit(solution)/shard_map/ppermute | solution.py:85
  13.2 2.4 %copy-start.7 = (s32[4]{0:T(128)S(1)}, s32[4]{0:T(128)}, u32[]{:S(2)}) copy-start(s32[4]{0:T(128)} %param.16) | copy-start | bytes 52
  13.2 3.2 %copy-start.6 = (f32[192]{0:T(256)S(1)}, f32[192]{0:T(256)}, u32[]{:S(2)}) copy-start(f32[192]{0:T(256)} %param.15) | copy-start | bytes 2308
  17.1 2.5 %slice-start.2 = ((bf16[3,3,3,384,384]{4,3,2,1,0:T(8,128)(2,1)}), bf16[2,3,3,384,384]{4,3,2,1,0:T(8,128)(2,1)S(1)}, s32[]{:S(2)}) async-start(bf16[3,3,3,384,384]{4,3,2,1,0:T(8,128)(2,1)} %param.12), calls=%async_computation.2 | async-start | bytes 10616832 | tf_op jit(solution)/shard_map/slice | solution.py:163
  19.6 3.0 %copy-start = (bf16[6,384,2,192]{1,0,3,2:T(8,128)(2,1)S(1)}, bf16[6,384,2,192]{1,0,3,2:T(8,128)(2,1)}, u32[]{:S(2)}) copy-start(bf16[6,384,2,192]{1,0,3,2:T(8,128)(2,1)} %get-tuple-element.18) | copy-start | bytes 5308420
  24.1 1.7 %copy-start.1 = (bf16[1,16,64,384]{3,2,1,0:T(8,128)(2,1)S(1)}, bf16[1,16,64,384]{3,2,1,0:T(8,128)(2,1)}, u32[]{:S(2)}) copy-start(bf16[1,16,64,384]{3,2,1,0:T(8,128)(2,1)} %param.10) | copy-start | bytes 2359300
  28.2 7.3 %collective-permute-start.5 = (bf16[1,1,384]{2,1,0:T(2,128)(2,1)S(1)}, bf16[1,1,384]{2,1,0:T(2,128)(2,1)S(1)}, u32[]{:S(2)}, u32[]{:S(2)}) collective-permute-start(bf16[1,1,384]{2,1,0:T(2,128)(2,1)S(1)} %constant_dynamic-slice_fusion.7), channel_id=1, source_target_pairs={{0,3},{4,7},{8,11},{12,15},{3,0},{7,4},{11,8},{15,12},{1,2},{5,6},... | collective-permute-start | bytes 2312 | tf_op jit(solution)/shard_map/ppermute | solution.py:85
  30.3 5.3 %collective-permute-start.6 = (bf16[1,64,384]{2,1,0:T(8,128)(2,1)S(1)}, bf16[1,64,384]{2,1,0:T(8,128)(2,1)S(1)}, u32[]{:S(2)}, u32[]{:S(2)}) collective-permute-start(bf16[1,64,384]{2,1,0:T(8,128)(2,1)S(1)} %constant_dynamic-slice_fusion.6), channel_id=1, source_target_pairs={{0,2},{1,3},{4,6},{5,7},{8,10},{9,11},{12,14},{13,15},{2,0},{3,1},... | collective-permute-start | bytes 147464 | tf_op jit(solution)/shard_map/ppermute | solution.py:85
  31.5 4.1 %collective-permute-start.7 = (bf16[16,1,384]{2,1,0:T(2,128)(2,1)S(1)}, bf16[16,1,384]{2,1,0:T(2,128)(2,1)S(1)}, u32[]{:S(2)}, u32[]{:S(2)}) collective-permute-start(bf16[16,1,384]{2,1,0:T(2,128)(2,1)S(1)} %constant_dynamic-slice_fusion.5), channel_id=1, source_target_pairs={{0,1},{2,3},{4,5},{6,7},{8,9},{10,11},{12,13},{14,15},{1,0},{3,2},... | collective-permute-start | bytes 36872 | tf_op jit(solution)/shard_map/ppermute | solution.py:85
  32.1 21.2 %collective-permute-start.1 = (bf16[16,64,384]{2,1,0:T(8,128)(2,1)}, bf16[16,64,384]{2,1,0:T(8,128)(2,1)S(1)}, u32[]{:S(2)}, u32[]{:S(2)}) collective-permute-start(bf16[16,64,384]{2,1,0:T(8,128)(2,1)} %collective-permute-done), channel_id=1, source_target_pairs={{0,4},{1,5},{2,6},{3,7},{4,8},{5,9},{6,10},{7,11},{8,12},{9,13},{1... | collective-permute-start | bytes 2359304 | tf_op jit(solution)/shard_map/ppermute | solution.py:25
  38.3 2.2 %slice-start.3 = ((s8[5308416]{0:T(1024)(128)(4,1)}), s8[4194304]{0:T(1024)(128)(4,1)S(1)}, s32[]{:S(2)}) async-start(s8[5308416]{0:T(1024)(128)(4,1)} %bitcast.94), calls=%async_computation.3 | async-start | bytes 8388608
  38.7 2.2 %slice-start.4 = ((s8[5308416]{0:T(1024)(128)(4,1)}), s8[1114112]{0:T(1024)(128)(4,1)S(1)}, s32[]{:S(2)}) async-start(s8[5308416]{0:T(1024)(128)(4,1)} %bitcast.94), calls=%async_computation.4 | async-start | bytes 2228224
  38.9 22.5 %slice-start = ((s8[7962624]{0:T(1024)(128)(4,1)}), s8[4194304]{0:T(1024)(128)(4,1)S(1)}, s32[]{:S(2)}) async-start(s8[7962624]{0:T(1024)(128)(4,1)} %bitcast.85), calls=%async_computation | async-start | bytes 8388608
  40.9 20.5 %slice-start.1 = ((s8[7962624]{0:T(1024)(128)(4,1)}), s8[3768320]{0:T(1024)(128)(4,1)S(1)}, s32[]{:S(2)}) async-start(s8[7962624]{0:T(1024)(128)(4,1)} %bitcast.85), calls=%async_computation.1 | async-start | bytes 7536640
  53.3 3.5 %collective-permute-start.2 = (bf16[1,1,384]{2,1,0:T(2,128)(2,1)S(1)}, bf16[1,1,384]{2,1,0:T(2,128)(2,1)S(1)}, u32[]{:S(2)}, u32[]{:S(2)}) collective-permute-start(bf16[1,1,384]{2,1,0:T(2,128)(2,1)S(1)} %constant_dynamic-slice_fusion.10), channel_id=1, source_target_pairs={{0,3},{4,7},{8,11},{12,15},{3,0},{7,4},{11,8},{15,12},{1,2},{5,6},... | collective-permute-start | bytes 2312 | tf_op jit(solution)/shard_map/ppermute | solution.py:85
  55.3 3.7 %collective-permute-start.3 = (bf16[1,64,384]{2,1,0:T(8,128)(2,1)S(1)}, bf16[1,64,384]{2,1,0:T(8,128)(2,1)S(1)}, u32[]{:S(2)}, u32[]{:S(2)}) collective-permute-start(bf16[1,64,384]{2,1,0:T(8,128)(2,1)S(1)} %constant_dynamic-slice_fusion.9), channel_id=1, source_target_pairs={{0,2},{1,3},{4,6},{5,7},{8,10},{9,11},{12,14},{13,15},{2,0},{3,1},... | collective-permute-start | bytes 147464 | tf_op jit(solution)/shard_map/ppermute | solution.py:85
  55.6 1.3 %collective-permute-start.4 = (bf16[16,1,384]{2,1,0:T(2,128)(2,1)S(1)}, bf16[16,1,384]{2,1,0:T(2,128)(2,1)S(1)}, u32[]{:S(2)}, u32[]{:S(2)}) collective-permute-start(bf16[16,1,384]{2,1,0:T(2,128)(2,1)S(1)} %constant_dynamic-slice_fusion.8), channel_id=1, source_target_pairs={{0,1},{2,3},{4,5},{6,7},{8,9},{10,11},{12,13},{14,15},{1,0},{3,2},... | collective-permute-start | bytes 36872 | tf_op jit(solution)/shard_map/ppermute | solution.py:85
  68.1 3.2 %collective-permute-start.11 = (bf16[1,1,384]{2,1,0:T(2,128)(2,1)S(1)}, bf16[1,1,384]{2,1,0:T(2,128)(2,1)S(1)}, u32[]{:S(2)}, u32[]{:S(2)}) collective-permute-start(bf16[1,1,384]{2,1,0:T(2,128)(2,1)S(1)} %constant_dynamic-slice_fusion.2), channel_id=1, source_target_pairs={{0,3},{4,7},{8,11},{12,15},{3,0},{7,4},{11,8},{15,12},{1,2},{5,6},... | collective-permute-start | bytes 2312 | tf_op jit(solution)/shard_map/ppermute | solution.py:85
  68.8 3.4 %collective-permute-start.12 = (bf16[1,64,384]{2,1,0:T(8,128)(2,1)S(1)}, bf16[1,64,384]{2,1,0:T(8,128)(2,1)S(1)}, u32[]{:S(2)}, u32[]{:S(2)}) collective-permute-start(bf16[1,64,384]{2,1,0:T(8,128)(2,1)S(1)} %constant_dynamic-slice_fusion.1), channel_id=1, source_target_pairs={{0,2},{1,3},{4,6},{5,7},{8,10},{9,11},{12,14},{13,15},{2,0},{3,1},... | collective-permute-start | bytes 147464 | tf_op jit(solution)/shard_map/ppermute | solution.py:85
  70.1 1.2 %collective-permute-start.13 = (bf16[16,1,384]{2,1,0:T(2,128)(2,1)S(1)}, bf16[16,1,384]{2,1,0:T(2,128)(2,1)S(1)}, u32[]{:S(2)}, u32[]{:S(2)}) collective-permute-start(bf16[16,1,384]{2,1,0:T(2,128)(2,1)S(1)} %constant_dynamic-slice_fusion), channel_id=1, source_target_pairs={{0,1},{2,3},{4,5},{6,7},{8,9},{10,11},{12,13},{14,15},{1,0},{3,2},... | collective-permute-start | bytes 36872 | tf_op jit(solution)/shard_map/ppermute | solution.py:85
  73.0 1.5 %copy-start.3 = (bf16[6,384,2,192]{1,3,2,0:T(8,128)(2,1)S(1)}, bf16[6,384,2,192]{1,3,2,0:T(8,128)(2,1)}, u32[]{:S(2)}) copy-start(bf16[6,384,2,192]{1,3,2,0:T(8,128)(2,1)} %copy.55) | copy-start | bytes 5308420
  (4 other events, 4.0 us)
